TPU v7x, 256 devices: a whole 4x4x8 slice. The times are simulated.
256 devices in a mesh: seq: 16 (over x, z_lo, core), hid: 16 (over z_hi, y).
Axes of the slice: x: 4, y: 4, z: 8 (z_hi: 4, z_lo: 2; z = z_hi * 2 + z_lo), core: 2. Of those that a mesh axis runs over, the one named last changes fastest.
Arguments:
- stream: bfloat16 [8192, 2048], P('seq'), may hold values from -5 to 5
- queries: bfloat16 [8192, 16, 128], P('seq', 'hid'), may hold values from -150 to 150
- key_rows: bfloat16 [8192, 16, 128], P('seq', 'hid'), may hold values from -5 to 5
- value_rows: bfloat16 [8192, 16, 128], P('seq', 'hid'), may hold values from -5 to 5
- segment_ids: int32 [8192], replicated, may hold values from 0 to 3, never falling along the last dimension, each value on 1 to 4096 neighbouring positions
- out_proj: bfloat16 [16, 128, 2048], P('hid'), may hold values from -0.125 to 0.125
- norm_gain: float32 [2048], replicated, may hold values from 0.1 to 1.9
- expert_ids: int32 [8192, 6], P('seq'), may hold values from 0 to 63, all different within a row; in each aligned block of 512 rows (0 to 511, 512 to 1023, ...) at most 64 rows name the same one
- route_gates: float32 [8192, 6], P('seq'), may hold values from 0.05 to 0.4
- gate_proj: bfloat16 [90112, 2048], P(('seq', 'hid')), may hold values from -0.125 to 0.125
- up_proj: bfloat16 [90112, 2048], P(('seq', 'hid')), may hold values from -0.125 to 0.125
- down_proj: bfloat16 [90112, 2048], P(('seq', 'hid')), may hold values from -0.15625 to 0.15625
- shared_gate: bfloat16 [2816, 2048], P('hid'), may hold values from -0.125 to 0.125
- shared_up: bfloat16 [2816, 2048], P('hid'), may hold values from -0.125 to 0.125
- shared_down: bfloat16 [2816, 2048], P('hid'), may hold values from -0.109375 to 0.109375
Outputs:
- layer_out: bfloat16 [8192, 2048], P('seq', 'hid')
Inputs may be any that keep to these rules, and one draw needn't show every extreme that they name: `segment_ids`: segment numbers never fall along the tokens; every segment has at most 4096 tokens and one has exactly 4096. `expert_ids`: the 6 experts of a token differ; among the 512 tokens of one index of seq no expert is named by more than 64 tokens, a bound that some block reaches of them.
All inputs are finite; a program needn't handle non-finite values.
Results may differ from a plain program's by a relative error of at most 0.019.
Values may be sent and summed in bfloat16 or wider, within the bound.
No kernel may reach another device: no remote copies, remote signals or barrier semaphores. Data moves between devices by JAX's collectives and lax.ppermute only.
A program may use at most 128 MiB of HBM per device.

v0:
```python
import jax
import jax.numpy as jnp
from jax import lax
from jax.sharding import PartitionSpec as P

EXPERTS = 64
FF = 1408
TOP = 6
CAP = 64
LONGEST = 4096


def seq_gather(rows, seq_count):
    spread = jnp.broadcast_to(rows[None], (seq_count,) + rows.shape)
    got = lax.all_to_all(spread, "seq", split_axis=0, concat_axis=0, tiled=True)
    return got.reshape((seq_count * rows.shape[0],) + rows.shape[1:])


def hid_scatter_sum(part, hid_count):
    rows, width = part.shape
    got = lax.all_to_all(
        part.reshape(rows, hid_count, width // hid_count),
        "hid",
        split_axis=1,
        concat_axis=1,
        tiled=True,
    )
    return jnp.sum(got.astype(jnp.float32), axis=1)


def hid_permute_sum(part, hid_count, hid_index):
    rows, width = part.shape
    chunks = part.reshape(rows, hid_count, width // hid_count)
    total = lax.dynamic_index_in_dim(chunks, hid_index, 1, keepdims=False).astype(jnp.float32)
    for shift in range(1, hid_count):
        sent = lax.dynamic_index_in_dim(chunks, (hid_index + shift) % hid_count, 1, keepdims=False)
        pairs = [(i, (i + shift) % hid_count) for i in range(hid_count)]
        total = total + lax.ppermute(sent, "hid", pairs).astype(jnp.float32)
    return total


def on_device(
    stream,
    queries,
    key_rows,
    value_rows,
    segment_ids,
    out_proj,
    norm_gain,
    expert_ids,
    route_gates,
    gate_proj,
    up_proj,
    down_proj,
    shared_gate,
    shared_up,
    shared_down,
):
    tok_count = queries.shape[0]
    local_heads = queries.shape[1]
    head_width = queries.shape[2]
    width = stream.shape[1]
    inv_root = head_width ** (-0.5)
    seq_count = lax.axis_size("seq")
    hid_count = lax.axis_size("hid")
    hid_index = lax.axis_index("hid")
    query_first = lax.axis_index("seq") * tok_count
    query_seg = lax.dynamic_slice_in_dim(segment_ids, query_first, tok_count)
    query_pos = query_first + jnp.arange(tok_count, dtype=jnp.int32)
    run_max = jnp.full((tok_count, local_heads), -1e30, jnp.float32)
    window = min(seq_count, -(-LONGEST // tok_count) + 1)
    both = jnp.concatenate([key_rows, value_rows], axis=1)
    blocks = [both]
    for shift in range(1, window):
        pairs = [(i, i + shift) for i in range(seq_count - shift)]
        blocks.append(lax.ppermute(both, "seq", pairs))
    both_win = jnp.concatenate(blocks[::-1], axis=0)
    key_part = both_win[:, :local_heads]
    value_part = both_win[:, local_heads:]
    row_count = key_part.shape[0]
    key_first = query_first - (window - 1) * tok_count
    key_pos = key_first + jnp.arange(row_count, dtype=jnp.int32)
    seg_padded = jnp.concatenate(
        [jnp.full(((window - 1) * tok_count,), -1, jnp.int32), segment_ids]
    )
    key_seg = lax.dynamic_slice_in_dim(seg_padded, query_first, row_count)
    scores = (
        jnp.einsum("qhd,khd->qhk", queries, key_part, preferred_element_type=jnp.float32) * inv_root
    )
    allowed = (query_seg[:, None] == key_seg[None, :]) & (key_pos[None, :] <= query_pos[:, None])
    scores = jnp.where(allowed[:, None, :], scores, -1e30)
    new_max = jnp.maximum(run_max, jnp.max(scores, axis=2))
    weights = jnp.where(allowed[:, None, :], jnp.exp(scores - new_max[:, :, None]), 0.0)
    new_sum = jnp.sum(weights, axis=2)
    probs = weights.astype(jnp.bfloat16)
    new_acc = jnp.einsum("qhk,khd->qhd", probs, value_part, preferred_element_type=jnp.float32)
    attended = (
        (new_acc / new_sum[:, :, None])
        .astype(jnp.bfloat16)
        .reshape(tok_count, local_heads * head_width)
    )
    out_flat = out_proj.reshape(local_heads * head_width, width)
    partial_mix = jnp.dot(attended, out_flat, preferred_element_type=jnp.float32)
    col_count = width // hid_count
    col_first = hid_index * col_count
    mixed_cols = lax.dynamic_slice_in_dim(stream, col_first, col_count, 1).astype(
        jnp.float32
    ) + hid_scatter_sum(partial_mix.astype(jnp.bfloat16), hid_count)
    mixed_all = (
        lax.all_to_all(
            jnp.broadcast_to(
                mixed_cols.astype(jnp.bfloat16)[:, None, :], (tok_count, hid_count, col_count)
            ),
            "hid",
            split_axis=1,
            concat_axis=1,
            tiled=True,
        )
        .reshape(tok_count, width)
        .astype(jnp.float32)
    )
    mean_square = jnp.mean(mixed_all * mixed_all, axis=1, keepdims=True)
    normed = (mixed_all * lax.rsqrt(mean_square + 1e-06) * norm_gain).astype(jnp.bfloat16)
    shared_gate_val = jnp.einsum(
        "td,fd->tf", normed, shared_gate, preferred_element_type=jnp.float32
    )
    shared_up_val = jnp.einsum("td,fd->tf", normed, shared_up, preferred_element_type=jnp.float32)
    shared_act = (jax.nn.silu(shared_gate_val) * shared_up_val).astype(jnp.bfloat16)
    shared_part = jnp.dot(shared_act, shared_down, preferred_element_type=jnp.float32)
    shared_out = hid_scatter_sum(shared_part.astype(jnp.bfloat16), hid_count)
    unit_rows = gate_proj.shape[0]
    held_count = max(1, unit_rows // FF)
    held_units = unit_rows // held_count
    local_experts = EXPERTS // seq_count
    first_local = hid_index * unit_rows // FF
    flat_ids = expert_ids.reshape(-1)
    onehot = (flat_ids[:, None] == jnp.arange(EXPERTS, dtype=jnp.int32)[None, :]).astype(jnp.int32)
    slot_rank = jnp.sum((jnp.cumsum(onehot, axis=0) - 1) * onehot, axis=1)
    owner_group = flat_ids // local_experts
    local_expert = flat_ids % local_experts
    held_offset = local_expert - first_local
    is_held = (held_offset >= 0) & (held_offset < held_count)
    slot_total = seq_count * held_count * CAP
    send_index = jnp.where(
        is_held, (owner_group * held_count + held_offset) * CAP + slot_rank, slot_total
    )
    route_token = jnp.arange(tok_count * TOP, dtype=jnp.int32) // TOP
    slot_token = jnp.full((slot_total,), -1, jnp.int32).at[send_index].set(route_token, mode="drop")
    send_rows = jnp.where(
        (slot_token >= 0)[:, None], normed[jnp.maximum(slot_token, 0)], jnp.zeros((), jnp.bfloat16)
    )
    send_rows = send_rows.reshape(seq_count, held_count, CAP, width)
    received = lax.all_to_all(send_rows, "seq", split_axis=0, concat_axis=0, tiled=True)
    gate_local = gate_proj.reshape(held_count, held_units, width)
    up_local = up_proj.reshape(held_count, held_units, width)
    down_local = down_proj.reshape(held_count, held_units, hid_count, col_count)
    gate_val = jnp.einsum(
        "sicd,ifd->sicf", received, gate_local, preferred_element_type=jnp.float32
    )
    up_val = jnp.einsum("sicd,ifd->sicf", received, up_local, preferred_element_type=jnp.float32)
    expert_act = (jax.nn.silu(gate_val) * up_val).astype(jnp.bfloat16)
    down_part = jnp.einsum(
        "sicf,ifnx->niscx", expert_act, down_local, preferred_element_type=jnp.float32
    ).astype(jnp.bfloat16)
    down_part = down_part.reshape(hid_count, held_count, seq_count * CAP, col_count)
    peer_parts = lax.all_to_all(down_part, "hid", split_axis=0, concat_axis=0, tiled=True)
    part_count = hid_count * held_count // local_experts
    expert_out = jnp.sum(
        peer_parts.reshape(local_experts, part_count, seq_count * CAP, col_count).astype(
            jnp.float32
        ),
        axis=1,
    ).astype(jnp.bfloat16)
    returned = lax.all_to_all(
        expert_out.reshape(local_experts, seq_count, CAP, col_count),
        "seq",
        split_axis=1,
        concat_axis=1,
        tiled=True,
    ).reshape(-1, col_count)
    pick_index = local_expert * (seq_count * CAP) + owner_group * CAP + slot_rank
    picked = returned[pick_index].reshape(tok_count, TOP, col_count)
    routed_sum = jnp.einsum("tj,tjd->td", route_gates, picked.astype(jnp.float32))
    return (mixed_cols + shared_out + routed_sum).astype(jnp.bfloat16)


def solution(mesh):
    placed = (
        P("seq", None),
        P("seq", "hid", None),
        P("seq", "hid", None),
        P("seq", "hid", None),
        P(),
        P("hid", None, None),
        P(),
        P("seq", None),
        P("seq", None),
        P(("seq", "hid"), None),
        P(("seq", "hid"), None),
        P(("seq", "hid"), None),
        P("hid", None),
        P("hid", None),
        P("hid", None),
    )
    return jax.shard_map(
        on_device, mesh=mesh, in_specs=placed, out_specs=P("seq", "hid"), check_vma=False
    )
```

profile of v0, /device:TPU:64, one launch (start us, length us, event | category | flops | bytes accessed | tf_op | source)
XLA Modules:
  0.0 507.8 jit_solution(17655521724245121680)
XLA Ops:
  0.0 1.0 constant_dynamic-update-slice_fusion.1
  1.1 1.0 constant_dynamic-update-slice_fusion
  2.0 4.9 collective-permute-start
  7.0 3.0 collective-permute-start.1
  10.0 2.1 collective-permute-start.2
  12.2 1.3 collective-permute-start.3
  13.5 1.6 collective-permute-start.4
  15.1 0.8 pad_dynamic-slice_fusion
  15.9 0.8 dynamic_slice.10
  16.7 8.2 %collective-permute-done = bf16[512,2,128]{2,0,1:T(8,128)(2,1)S(1)} collective-permute-done((bf16[512,2,128]{2,0,1:T(8,128)(2,1)S(1)}, bf16[512,2,128]{2,0,1:T(8,128)(2,1)S(1)}, u32[]{:S(2)}, u32[]{:S(2)}) %collective-permute-start) | collective-permute-done | bytes 262176 | tf_op jit(solution)/shard_map/ppermute | solution.py:76
  24.9 2.0 collective-permute-start.5
  27.0 3.9 collective-permute-start.6
  30.9 3.8 collective-permute-start.7
  34.7 7.1 %collective-permute-done.3 = bf16[512,2,128]{2,0,1:T(8,128)(2,1)S(1)} collective-permute-done((bf16[512,2,128]{2,0,1:T(8,128)(2,1)S(1)}, bf16[512,2,128]{2,0,1:T(8,128)(2,1)S(1)}, u32[]{:S(2)}, u32[]{:S(2)}) %collective-permute-start.3) | collective-permute-done | bytes 262176 | tf_op jit(solution)/shard_map/ppermute | solution.py:76
  41.8 5.6 %collective-permute-done.4 = bf16[512,2,128]{2,0,1:T(8,128)(2,1)S(1)} collective-permute-done((bf16[512,2,128]{2,0,1:T(8,128)(2,1)S(1)}, bf16[512,2,128]{2,0,1:T(8,128)(2,1)S(1)}, u32[]{:S(2)}, u32[]{:S(2)}) %collective-permute-start.4) | collective-permute-done | bytes 262176 | tf_op jit(solution)/shard_map/ppermute | solution.py:76
  47.7 2.2 fusion
  49.9 3.6 copy-done.2
  53.5 4.1 fusion.1
  57.6 8.1 %fusion.13 = bf16[64,16,8,128]{3,2,1,0:T(8,128)(2,1)S(1)} fusion(f32[4608,512]{1,0:T(8,128)} %copy-done.2, f32[512]{0:T(512)S(1)} %broadcast_maximum_fusion, s32[512]{0:T(512)S(1)} %iota_add_fusion.1, s32[512]{0:T(512)S(1)} %dynamic_slice.10, s32[4608]{0:T(1024)} %copy-done.11, s32[4608]{0:T(1024)} %copy-done.10, bf16[4608,2,128]{2,0,1:T(8,128)(2,1)} %copy-done.14, ...), kind=kOutput, calls=%fused_computation.30 | convolution fusion | flops 892469248 | bytes 13287424 | tf_op jit(solution)/shard_map/dot_general | solution.py:103
  65.7 1.9 copy.69
  67.6 10.8 %all-to-all-start = ((bf16[512,16,128]{2,0,1:T(8,128)(2,1)}), bf16[512,16,128]{2,0,1:T(8,128)(2,1)S(1)}, u32[]{:S(2)}, u32[]{:S(2)}) async-start(bf16[512,16,128]{2,0,1:T(8,128)(2,1)} %bitcast.219), calls=%async_computation | async-start | bytes 4194304 | tf_op jit(solution)/shard_map/all_to_all | solution.py:21
  78.3 44.6 %all-to-all-done = bf16[512,16,128]{2,0,1:T(8,128)(2,1)S(1)} async-done(((bf16[512,16,128]{2,0,1:T(8,128)(2,1)}), bf16[512,16,128]{2,0,1:T(8,128)(2,1)S(1)}, u32[]{:S(2)}, u32[]{:S(2)}) %all-to-all-start) | async-done | bytes 2097184 | tf_op jit(solution)/shard_map/all_to_all | solution.py:21
  123.9 0.9 fusion.59
  124.9 1.7 broadcast_in_dim.58
  126.6 8.0 %all-to-all-start.1 = ((bf16[512,16,128]{2,0,1:T(8,128)(2,1)}), bf16[512,16,128]{2,0,1:T(8,128)(2,1)S(1)}, u32[]{:S(2)}, u32[]{:S(2)}) async-start(bf16[512,16,128]{2,0,1:T(8,128)(2,1)} %broadcast_in_dim.58), calls=%async_computation.1 | async-start | bytes 4194304 | tf_op jit(solution)/shard_map/all_to_all | solution.py:110
  134.6 0.9 copy.40
  135.4 1.7 eq.54
  137.1 1.7 eq.50
  138.9 1.1 reshape.403
  140.0 1.6 fusion.50
  141.6 34.8 %reduce-window.6 = s32[64,24,128]{2,1,0:T(8,128)} reduce-window(s32[64,24,128]{2,1,0:T(8,128)} %fusion.50, s32[]{:T(128)} %constant.41.clone.1), window={size=1x1x128 pad=0_0x0_0x127_0}, to_apply=%region_5.6 | reduce-window | flops 24969216 | bytes 1572868 | tf_op jit(solution)/shard_map/reduce-window
  176.5 2.3 slice.22
  178.8 2.2 copy.54
  181.0 1.6 reduce-window.9
  183.1 1.4 add_add_fusion
  184.5 0.9 fusion.48
  186.2 12.1 %scatter_custom_fusion = s32[1024]{0:T(1024)S(1)} fusion(s32[3072]{0:T(1024)S(1)} %bitcast.230, s32[3072]{0:T(1024)} %add_select_fusion, s32[]{:T(128)} %constant.86.clone.1), kind=kCustom, calls=%fused_computation.105 | custom fusion | bytes 4608 | tf_op jit(solution)/shard_map/scatter | solution.py:148
  198.9 0.8 copy-done.1
  199.8 2.1 fusion.8
  201.9 6.0 %gather_fusion = bf16[1024,2048]{1,0:T(8,128)(2,1)} fusion(bf16[512,2048]{1,0:T(8,128)(2,1)S(1)} %fusion.8, s32[1024]{0:T(1024)S(1)} %maximum_clamp_fusion), kind=kCustom, calls=%fused_computation | custom fusion | bytes 8392704 | tf_op jit(solution)/shard_map/gather | solution.py:150
  207.9 2.5 broadcast_select_fusion
  210.5 56.2 %all_to_all.30 = bf16[16,1,64,2048]{3,2,1,0:T(8,128)(2,1)S(1)} all-to-all(bf16[16,1,64,2048]{3,2,1,0:T(8,128)(2,1)S(1)} %broadcast_select_fusion), channel_id=1, replica_groups=mesh['seq'=16,'hid'=16] {'seq'}, dimensions={0} | all-to-all | bytes 8388608 | tf_op jit(solution)/shard_map/all_to_all | solution.py:153
  266.7 1.9 copy-done.3
  268.6 3.5 fusion.11
  272.2 8.4 %convert_bitcast_fusion.1 = bf16[16,1,16,64,128]{4,3,0,2,1:T(8,128)(2,1)} fusion(bf16[352,2048]{1,0:T(8,128)(2,1)S(1)} %copy-done, bf16[16,1,64,2048]{3,2,1,0:T(8,128)(2,1)} %copy-done.3, f32[16,64,352]{2,1,0:T(8,128)} %fusion.11, bf16[352,2048]{1,0:T(8,128)(2,1)} %param.26), kind=kOutput, calls=%fused_computation.22 | convolution fusion | flops 2957049856 | bytes 12713984 | tf_op jit(solution)/shard_map/sicf,ifnx->niscx/dot_general | solution.py:162
  280.6 5.5 %copy.47 = bf16[16,1,16,64,128]{4,3,2,0,1:T(8,128)(2,1)} copy(bf16[16,1,16,64,128]{4,3,0,2,1:T(8,128)(2,1)} %convert_bitcast_fusion.1) | data formatting | bytes 8388608 | tf_op jit(solution)/shard_map/convert_element_type | solution.py:164
  286.1 9.6 %all-to-all-start.4 = ((bf16[16,1,1024,128]{3,2,1,0:T(8,128)(2,1)}), bf16[16,1,1024,128]{3,2,1,0:T(8,128)(2,1)}, u32[]{:S(2)}, u32[]{:S(2)}) async-start(bf16[16,1,1024,128]{3,2,1,0:T(8,128)(2,1)} %bitcast.218), calls=%async_computation.4 | async-start | bytes 8388608 | tf_op jit(solution)/shard_map/all_to_all | solution.py:166
  295.7 2.7 fusion.76
  298.4 4.4 fusion.14
  302.8 3.5 copy.68
  306.3 78.1 %all-to-all-done.4 = bf16[16,1,1024,128]{3,2,1,0:T(8,128)(2,1)} async-done(((bf16[16,1,1024,128]{3,2,1,0:T(8,128)(2,1)}), bf16[16,1,1024,128]{3,2,1,0:T(8,128)(2,1)}, u32[]{:S(2)}, u32[]{:S(2)}) %all-to-all-start.4) | async-done | bytes 4194336 | tf_op jit(solution)/shard_map/all_to_all | solution.py:166
  384.5 13.2 %all-to-all-start.2 = ((bf16[512,16,128]{2,0,1:T(8,128)(2,1)}), bf16[512,16,128]{2,0,1:T(8,128)(2,1)S(1)}, u32[]{:S(2)}, u32[]{:S(2)}) async-start(bf16[512,16,128]{2,0,1:T(8,128)(2,1)} %bitcast.220), calls=%async_computation.2 | async-start | bytes 4194304 | tf_op jit(solution)/shard_map/all_to_all | solution.py:21
  397.6 2.9 bitcast_reduce_fusion
  400.5 1.1 copy.49
  401.6 28.3 %all-to-all-done.2 = bf16[512,16,128]{2,0,1:T(8,128)(2,1)S(1)} async-done(((bf16[512,16,128]{2,0,1:T(8,128)(2,1)}), bf16[512,16,128]{2,0,1:T(8,128)(2,1)S(1)}, u32[]{:S(2)}, u32[]{:S(2)}) %all-to-all-start.2) | async-done | bytes 2097184 | tf_op jit(solution)/shard_map/all_to_all | solution.py:21
  429.8 46.1 %all-to-all-start.5 = ((bf16[4,16,64,128]{3,2,0,1:T(8,128)(2,1)}), bf16[4,16,64,128]{3,2,0,1:T(8,128)(2,1)}, u32[]{:S(2)}, u32[]{:S(2)}) async-start(bf16[4,16,64,128]{3,2,0,1:T(8,128)(2,1)} %copy.49), calls=%async_computation.5 | async-start | bytes 2097152 | tf_op jit(solution)/shard_map/all_to_all | solution.py:174
  476.0 1.7 copy.52
  478.3 1.0 convert_reduce_fusion
  479.2 13.3 %all-to-all-done.5 = bf16[4,16,64,128]{3,2,0,1:T(8,128)(2,1)} async-done(((bf16[4,16,64,128]{3,2,0,1:T(8,128)(2,1)}), bf16[4,16,64,128]{3,2,0,1:T(8,128)(2,1)}, u32[]{:S(2)}, u32[]{:S(2)}) %all-to-all-start.5) | async-done | bytes 1048608 | tf_op jit(solution)/shard_map/all_to_all | solution.py:174
  492.6 1.3 copy.50
  493.9 9.2 %gather_fusion.1 = bf16[3072,128]{1,0:T(8,128)(2,1)S(1)} fusion(bf16[4096,128]{1,0:T(8,128)(2,1)S(1)} %bitcast.216, s32[3072]{0:T(1024)S(1)} %copy-done.13), kind=kCustom, calls=%fused_computation.1 | custom fusion | bytes 1585152 | tf_op jit(solution)/shard_map/gather | solution.py:182
  503.1 1.2 reshape.412
  504.3 1.9 fusion.77
  506.2 1.6 add_convert_fusion
  (61 shorter events, 3.9 us)
Async XLA Ops:
  0.0 272.2 %copy-start = (bf16[352,2048]{1,0:T(8,128)(2,1)S(1)}, bf16[352,2048]{1,0:T(8,128)(2,1)}, u32[]{:S(2)}) copy-start(bf16[352,2048]{1,0:T(8,128)(2,1)} %param.25) | copy-start | bytes 4325380
  0.0 47.6 %copy-start.7 = (bf16[512,1,128]{2,0,1:T(8,128)(2,1)S(1)}, bf16[512,1,128]{2,0,1:T(8,128)(2,1)}, u32[]{:S(2)}) copy-start(bf16[512,1,128]{2,0,1:T(8,128)(2,1)} %param.17) | copy-start | bytes 393220
  1.0 46.6 %copy-start.8 = (bf16[512,1,128]{2,0,1:T(8,128)(2,1)S(1)}, bf16[512,1,128]{2,0,1:T(8,128)(2,1)}, u32[]{:S(2)}) copy-start(bf16[512,1,128]{2,0,1:T(8,128)(2,1)} %param.18) | copy-start | bytes 393220
  2.0 22.9 %collective-permute-start = (bf16[512,2,128]{2,0,1:T(8,128)(2,1)S(1)}, bf16[512,2,128]{2,0,1:T(8,128)(2,1)S(1)}, u32[]{:S(2)}, u32[]{:S(2)}) collective-permute-start(bf16[512,2,128]{2,0,1:T(8,128)(2,1)S(1)} %constant_dynamic-update-slice_fusion), channel_id=1, source_target_pairs={{0,128},{16,144},{32,160},{48,176},{64,192},{80,208},{96,224},{112... | collective-permute-start | bytes 786440 | tf_op jit(solution)/shard_map/ppermute | solution.py:76
  7.0 20.0 %collective-permute-start.1 = (bf16[512,2,128]{2,0,1:T(8,128)(2,1)S(1)}, bf16[512,2,128]{2,0,1:T(8,128)(2,1)S(1)}, u32[]{:S(2)}, u32[]{:S(2)}) collective-permute-start(bf16[512,2,128]{2,0,1:T(8,128)(2,1)S(1)} %constant_dynamic-update-slice_fusion), channel_id=1, source_target_pairs={{0,112},{16,128},{32,144},{48,160},{64,176},{80,192},{96,208},{112... | collective-permute-start | bytes 786440 | tf_op jit(solution)/shard_map/ppermute | solution.py:76
  10.0 20.9 %collective-permute-start.2 = (bf16[512,2,128]{2,0,1:T(8,128)(2,1)S(1)}, bf16[512,2,128]{2,0,1:T(8,128)(2,1)S(1)}, u32[]{:S(2)}, u32[]{:S(2)}) collective-permute-start(bf16[512,2,128]{2,0,1:T(8,128)(2,1)S(1)} %constant_dynamic-update-slice_fusion), channel_id=1, source_target_pairs={{0,96},{16,112},{32,128},{48,144},{64,160},{80,176},{96,192},{112,... | collective-permute-start | bytes 786440 | tf_op jit(solution)/shard_map/ppermute | solution.py:76
  12.2 29.6 %collective-permute-start.3 = (bf16[512,2,128]{2,0,1:T(8,128)(2,1)S(1)}, bf16[512,2,128]{2,0,1:T(8,128)(2,1)S(1)}, u32[]{:S(2)}, u32[]{:S(2)}) collective-permute-start(bf16[512,2,128]{2,0,1:T(8,128)(2,1)S(1)} %constant_dynamic-update-slice_fusion), channel_id=1, source_target_pairs={{0,80},{16,96},{32,112},{48,128},{64,144},{80,160},{96,176},{112,1... | collective-permute-start | bytes 786440 | tf_op jit(solution)/shard_map/ppermute | solution.py:76
  13.5 33.9 %collective-permute-start.4 = (bf16[512,2,128]{2,0,1:T(8,128)(2,1)S(1)}, bf16[512,2,128]{2,0,1:T(8,128)(2,1)S(1)}, u32[]{:S(2)}, u32[]{:S(2)}) collective-permute-start(bf16[512,2,128]{2,0,1:T(8,128)(2,1)S(1)} %constant_dynamic-update-slice_fusion), channel_id=1, source_target_pairs={{0,64},{16,80},{32,96},{48,112},{64,128},{80,144},{96,160},{112,17... | collective-permute-start | bytes 786440 | tf_op jit(solution)/shard_map/ppermute | solution.py:76
  15.9 34.0 %copy-start.10 = (s32[4608]{0:T(1024)}, s32[4608]{0:T(1024)S(1)}, u32[]{:S(2)}) copy-start(s32[4608]{0:T(1024)S(1)} %get-tuple-element.10) | copy-start | bytes 55300
  15.9 34.0 %copy-start.11 = (s32[4608]{0:T(1024)}, s32[4608]{0:T(1024)S(1)}, u32[]{:S(2)}) copy-start(s32[4608]{0:T(1024)S(1)} %get-tuple-element.11) | copy-start | bytes 55300
  16.7 31.0 %copy-start.17 = (bf16[512,1,128]{2,0,1:T(8,128)(2,1)S(1)}, bf16[512,1,128]{2,0,1:T(8,128)(2,1)}, u32[]{:S(2)}) copy-start(bf16[512,1,128]{2,0,1:T(8,128)(2,1)} %param.16) | copy-start | bytes 393220
  24.9 22.5 %collective-permute-start.5 = (bf16[512,2,128]{2,0,1:T(8,128)(2,1)S(1)}, bf16[512,2,128]{2,0,1:T(8,128)(2,1)S(1)}, u32[]{:S(2)}, u32[]{:S(2)}) collective-permute-start(bf16[512,2,128]{2,0,1:T(8,128)(2,1)S(1)} %constant_dynamic-update-slice_fusion), channel_id=1, source_target_pairs={{0,48},{16,64},{32,80},{48,96},{64,112},{80,128},{96,144},{112,160... | collective-permute-start | bytes 786440 | tf_op jit(solution)/shard_map/ppermute | solution.py:76
  27.0 20.5 %collective-permute-start.6 = (bf16[512,2,128]{2,0,1:T(8,128)(2,1)S(1)}, bf16[512,2,128]{2,0,1:T(8,128)(2,1)S(1)}, u32[]{:S(2)}, u32[]{:S(2)}) collective-permute-start(bf16[512,2,128]{2,0,1:T(8,128)(2,1)S(1)} %constant_dynamic-update-slice_fusion), channel_id=1, source_target_pairs={{0,32},{16,48},{32,64},{48,80},{64,96},{80,112},{96,128},{112,144}... | collective-permute-start | bytes 786440 | tf_op jit(solution)/shard_map/ppermute | solution.py:76
  30.9 16.7 %collective-permute-start.7 = (bf16[512,2,128]{2,0,1:T(8,128)(2,1)S(1)}, bf16[512,2,128]{2,0,1:T(8,128)(2,1)S(1)}, u32[]{:S(2)}, u32[]{:S(2)}) collective-permute-start(bf16[512,2,128]{2,0,1:T(8,128)(2,1)S(1)} %constant_dynamic-update-slice_fusion), channel_id=1, source_target_pairs={{0,16},{16,32},{32,48},{48,64},{64,80},{80,96},{96,112},{112,128},... | collective-permute-start | bytes 786440 | tf_op jit(solution)/shard_map/ppermute | solution.py:76
  47.7 2.2 copy-start.14
  49.9 3.6 copy-start.2
  67.6 55.4 %all-to-all-start = ((bf16[512,16,128]{2,0,1:T(8,128)(2,1)}), bf16[512,16,128]{2,0,1:T(8,128)(2,1)S(1)}, u32[]{:S(2)}, u32[]{:S(2)}) async-start(bf16[512,16,128]{2,0,1:T(8,128)(2,1)} %bitcast.219), calls=%async_computation | async-start | bytes 4194304 | tf_op jit(solution)/shard_map/all_to_all | solution.py:21
  123.2 0.7 copy-start.4
  126.6 8.0 %copy-start.15 = (s32[512,6]{0,1:T(8,128)S(1)}, s32[512,6]{0,1:T(8,128)}, u32[]{:S(2)}) copy-start(s32[512,6]{0,1:T(8,128)} %param.22) | copy-start | bytes 36868
  126.6 71.8 %all-to-all-start.1 = ((bf16[512,16,128]{2,0,1:T(8,128)(2,1)}), bf16[512,16,128]{2,0,1:T(8,128)(2,1)S(1)}, u32[]{:S(2)}, u32[]{:S(2)}) async-start(bf16[512,16,128]{2,0,1:T(8,128)(2,1)} %broadcast_in_dim.58), calls=%async_computation.1 | async-start | bytes 4194304 | tf_op jit(solution)/shard_map/all_to_all | solution.py:110
  198.4 1.3 copy-start.1
  210.5 58.1 %copy-start.16 = (bf16[352,2048]{1,0:T(8,128)(2,1)S(1)}, bf16[352,2048]{1,0:T(8,128)(2,1)}, u32[]{:S(2)}) copy-start(bf16[352,2048]{1,0:T(8,128)(2,1)} %param.24) | copy-start | bytes 4325380
  266.7 1.9 copy-start.3
  286.1 98.4 %all-to-all-start.4 = ((bf16[16,1,1024,128]{3,2,1,0:T(8,128)(2,1)}), bf16[16,1,1024,128]{3,2,1,0:T(8,128)(2,1)}, u32[]{:S(2)}, u32[]{:S(2)}) async-start(bf16[16,1,1024,128]{3,2,1,0:T(8,128)(2,1)} %bitcast.218), calls=%async_computation.4 | async-start | bytes 8388608 | tf_op jit(solution)/shard_map/all_to_all | solution.py:166
  384.5 45.4 %all-to-all-start.2 = ((bf16[512,16,128]{2,0,1:T(8,128)(2,1)}), bf16[512,16,128]{2,0,1:T(8,128)(2,1)S(1)}, u32[]{:S(2)}, u32[]{:S(2)}) async-start(bf16[512,16,128]{2,0,1:T(8,128)(2,1)} %bitcast.220), calls=%async_computation.2 | async-start | bytes 4194304 | tf_op jit(solution)/shard_map/all_to_all | solution.py:21
  400.5 77.2 %copy-start.12 = (s32[3072,1]{0,1:T(1,128)S(1)}, s32[3072,1]{0,1:T(1,128)}, u32[]{:S(2)}) copy-start(s32[3072,1]{0,1:T(1,128)} %get-tuple-element.5) | copy-start | bytes 36868
  429.8 62.7 %all-to-all-start.5 = ((bf16[4,16,64,128]{3,2,0,1:T(8,128)(2,1)}), bf16[4,16,64,128]{3,2,0,1:T(8,128)(2,1)}, u32[]{:S(2)}, u32[]{:S(2)}) async-start(bf16[4,16,64,128]{3,2,0,1:T(8,128)(2,1)} %copy.49), calls=%async_computation.5 | async-start | bytes 2097152 | tf_op jit(solution)/shard_map/all_to_all | solution.py:174
  478.3 15.6 %copy-start.13 = (s32[3072]{0:T(1024)S(1)}, s32[3072]{0:T(1024)}, u32[]{:S(2)}) copy-start(s32[3072]{0:T(1024)} %broadcast_clamp_fusion) | copy-start | bytes 36868
  493.9 10.4 %copy-start.9 = (bf16[512,6,1]{1,2,0:T(2,128)(2,1)S(1)}, bf16[512,6,1]{1,2,0:T(2,128)(2,1)}, u32[]{:S(2)}) copy-start(bf16[512,6,1]{1,2,0:T(2,128)(2,1)} %copy.52) | copy-start | bytes 18436
  503.1 3.2 copy-start.5
  503.1 3.2 copy-start.6
where the time goes:
time: 512 us; the launch traced here: 508 us
  waiting for transfers between devices  185 us (36%)
  starting transfers between devices  110 us (21%)
  local copies, waits for them, and re-layouts  65.4 us (13%)
  other arithmetic  59.1 us (12%)
  blocking collectives  56.2 us (11%)
  matrix products  31.2 us (6%)
    all_to_all x1, waiting for transfers between devices, on_device(): lax.all_to_all(down_part, 'hid', split_axis=0, concat_axis=0, tiled=True)  78.1 us
    all_to_all x2, waiting for transfers between devices, hid_scatter_sum(): lax.all_to_all(part.reshape(rows, hid_count, width // hid_count), 'hid',...  72.9 us
    all_to_all x1, blocking collectives, on_device(): lax.all_to_all(send_rows, 'seq', split_axis=0, concat_axis=0, tiled=True)  56.2 us
    all_to_all x1, starting transfers between devices, on_device(): lax.all_to_all(expert_out.reshape(local_experts, seq_count, CAP, col_coun...  46.1 us
    another operation x2, other arithmetic  36.4 us
    all_to_all x2, starting transfers between devices, hid_scatter_sum(): lax.all_to_all(part.reshape(rows, hid_count, width // hid_count), 'hid',...  23.9 us
    ppermute x8, starting transfers between devices, on_device(): blocks.append(lax.ppermute(both, 'seq', pairs))  22.6 us
    ppermute x8, waiting for transfers between devices, on_device(): blocks.append(lax.ppermute(both, 'seq', pairs))  20.9 us
  transfers between devices with their start and end apart: 13, of which 7 were waited for; matrix products, arithmetic and copies ran while one was open for 16% of the time, Pallas kernels for 0%

commit v1 on v0

--- a/solution.py
+++ b/solution.py
@@ -18,12 +18,18 @@
 
 def hid_scatter_sum(part, hid_count):
     rows, width = part.shape
-    got = lax.all_to_all(
-        part.reshape(rows, hid_count, width // hid_count),
-        "hid",
-        split_axis=1,
-        concat_axis=1,
-        tiled=True,
+    got = jnp.concatenate(
+        lax.all_to_all(
+            jnp.stack(
+                jnp.split(
+                    part.reshape(rows, hid_count, width // hid_count), lax.axis_size("hid"), axis=1
+                )
+            ),
+            "hid",
+            0,
+            0,
+        ),
+        axis=1,
     )
     return jnp.sum(got.astype(jnp.float32), axis=1)
 

time: 512 us -> 527 us (1.029)
  local copies, waits for them, and re-layouts: 65.4 us -> 84.9 us
    unnamed x48 -> x86, local copies, waits for them, and re-layouts: 11 us -> 25.7 us
    split x0 -> x2, local copies, waits for them, and re-layouts: none -> 9.16 us  [hid_scatter_sum(): jnp.split(part.reshape(rows, hid_count, width // hid_count), lax.axis_siz...]
    reshape x2 -> x0, local copies, waits for them, and re-layouts: 5.37 us -> none  [hid_scatter_sum(): part.reshape(rows, hid_count, width // hid_count)]
    all_to_all x1, waiting for transfers between devices: 78.1 us -> 72.9 us  [on_device(): lax.all_to_all(down_part, 'hid', split_axis=0, concat_axis=0, tiled=True)]
  transfers between devices with their start and end apart: 13 -> 13, of which waited for: 7 -> 7; matrix products, arithmetic and copies ran while one was open for 16% -> 17% of each run, Pallas kernels for 0% -> 0%
where the time goes in v1:
time: 527 us; the launch traced here: 522 us
  waiting for transfers between devices  181 us (34%)
  starting transfers between devices  110 us (21%)
  local copies, waits for them, and re-layouts  84.9 us (16%)
  other arithmetic  59 us (11%)
  blocking collectives  55.9 us (11%)
  matrix products  31.2 us (6%)
    all_to_all x2, waiting for transfers between devices, hid_scatter_sum(): lax.all_to_all(jnp.stack(jnp.split(part.reshape(rows, hid_count, width //...  73.6 us
    all_to_all x1, waiting for transfers between devices, on_device(): lax.all_to_all(down_part, 'hid', split_axis=0, concat_axis=0, tiled=True)  72.9 us
    all_to_all x1, blocking collectives, on_device(): lax.all_to_all(send_rows, 'seq', split_axis=0, concat_axis=0, tiled=True)  55.9 us
    all_to_all x1, starting transfers between devices, on_device(): lax.all_to_all(expert_out.reshape(local_experts, seq_count, CAP, col_coun...  46.1 us
    another operation x2, other arithmetic  36.3 us
    unnamed x86, local copies, waits for them, and re-layouts  25.7 us
    all_to_all x2, starting transfers between devices, hid_scatter_sum(): lax.all_to_all(jnp.stack(jnp.split(part.reshape(rows, hid_count, width //...  23.9 us
    ppermute x8, starting transfers between devices, on_device(): blocks.append(lax.ppermute(both, 'seq', pairs))  22.6 us
  transfers between devices with their start and end apart: 13, of which 7 were waited for; matrix products, arithmetic and copies ran while one was open for 17% of the time, Pallas kernels for 0%

profile of v1, /device:TPU:64, one launch (start us, length us, event | category | flops | bytes accessed | tf_op | source)
XLA Modules:
  0.0 522.1 jit_solution(1454931714254336892)
XLA Ops:
  0.0 1.0 constant_dynamic-update-slice_fusion.1
  1.0 0.9 constant_dynamic-update-slice_fusion
  2.0 4.9 collective-permute-start
  6.9 3.0 collective-permute-start.1
  9.9 2.1 collective-permute-start.2
  12.1 1.3 collective-permute-start.3
  13.4 1.6 collective-permute-start.4
  16.6 8.2 %collective-permute-done = bf16[512,2,128]{2,0,1:T(8,128)(2,1)S(1)} collective-permute-done((bf16[512,2,128]{2,0,1:T(8,128)(2,1)S(1)}, bf16[512,2,128]{2,0,1:T(8,128)(2,1)S(1)}, u32[]{:S(2)}, u32[]{:S(2)}) %collective-permute-start) | collective-permute-done | bytes 262176 | tf_op jit(solution)/shard_map/ppermute | solution.py:82
  24.8 2.0 collective-permute-start.5
  26.9 4.0 collective-permute-start.6
  31.0 3.6 collective-permute-start.7
  34.6 7.1 %collective-permute-done.3 = bf16[512,2,128]{2,0,1:T(8,128)(2,1)S(1)} collective-permute-done((bf16[512,2,128]{2,0,1:T(8,128)(2,1)S(1)}, bf16[512,2,128]{2,0,1:T(8,128)(2,1)S(1)}, u32[]{:S(2)}, u32[]{:S(2)}) %collective-permute-start.3) | collective-permute-done | bytes 262176 | tf_op jit(solution)/shard_map/ppermute | solution.py:82
  41.7 5.6 %collective-permute-done.4 = bf16[512,2,128]{2,0,1:T(8,128)(2,1)S(1)} collective-permute-done((bf16[512,2,128]{2,0,1:T(8,128)(2,1)S(1)}, bf16[512,2,128]{2,0,1:T(8,128)(2,1)S(1)}, u32[]{:S(2)}, u32[]{:S(2)}) %collective-permute-start.4) | collective-permute-done | bytes 262176 | tf_op jit(solution)/shard_map/ppermute | solution.py:82
  47.6 2.2 fusion
  49.8 3.6 copy-done.2
  53.4 4.1 fusion.1
  57.6 8.1 %fusion.13 = bf16[64,8,16,128]{3,1,2,0:T(8,128)(2,1)S(1)} fusion(f32[4608,512]{1,0:T(8,128)} %copy-done.2, f32[512]{0:T(512)S(1)} %broadcast_maximum_fusion, s32[512]{0:T(512)S(1)} %iota_add_fusion.1, s32[512]{0:T(512)S(1)} %dynamic_slice.10, s32[4608]{0:T(1024)} %copy-done.12, s32[4608]{0:T(1024)} %copy-done.11, bf16[4608,2,128]{2,0,1:T(8,128)(2,1)} %copy-done.15, ...), kind=kOutput, calls=%fused_computation.28 | convolution fusion | flops 892469248 | bytes 13287424 | tf_op jit(solution)/shard_map/dot_general | solution.py:109
  66.2 4.6 fusion.109
  81.5 10.8 %all-to-all-start = ((bf16[16,512,1,128]{3,1,2,0:T(8,128)(2,1)}), bf16[16,512,1,128]{3,1,2,0:T(8,128)(2,1)S(1)}, u32[]{:S(2)}, u32[]{:S(2)}) async-start(bf16[16,512,1,128]{3,1,2,0:T(8,128)(2,1)} %fusion.77), calls=%async_computation | async-start | bytes 4194304 | tf_op jit(solution)/shard_map/all_to_all | solution.py:22
  92.3 45.3 %all-to-all-done = bf16[16,512,1,128]{3,1,2,0:T(8,128)(2,1)S(1)} async-done(((bf16[16,512,1,128]{3,1,2,0:T(8,128)(2,1)}), bf16[16,512,1,128]{3,1,2,0:T(8,128)(2,1)S(1)}, u32[]{:S(2)}, u32[]{:S(2)}) %all-to-all-start) | async-done | bytes 2097184 | tf_op jit(solution)/shard_map/all_to_all | solution.py:22
  138.6 0.9 fusion.59
  139.5 1.7 broadcast_in_dim.58
  141.3 7.4 %all-to-all-start.1 = ((bf16[512,16,128]{2,0,1:T(8,128)(2,1)}), bf16[512,16,128]{2,0,1:T(8,128)(2,1)S(1)}, u32[]{:S(2)}, u32[]{:S(2)}) async-start(bf16[512,16,128]{2,0,1:T(8,128)(2,1)} %broadcast_in_dim.58), calls=%async_computation.1 | async-start | bytes 4194304 | tf_op jit(solution)/shard_map/all_to_all | solution.py:116
  148.7 0.9 copy.162
  149.6 1.7 eq.54
  151.3 1.7 eq.50
  153.0 1.1 reshape.409
  154.2 1.6 fusion.50
  155.8 34.8 %reduce-window.6 = s32[64,24,128]{2,1,0:T(8,128)} reduce-window(s32[64,24,128]{2,1,0:T(8,128)} %fusion.50, s32[]{:T(128)} %constant.41.clone.1), window={size=1x1x128 pad=0_0x0_0x127_0}, to_apply=%region_5.6 | reduce-window | flops 24969216 | bytes 1572868 | tf_op jit(solution)/shard_map/reduce-window
  190.6 2.3 slice.22
  192.9 2.2 copy.176
  195.1 1.5 reduce-window.9
  197.2 1.4 add_add_fusion
  198.6 0.9 fusion.48
  200.3 11.9 %scatter_custom_fusion = s32[1024]{0:T(1024)S(1)} fusion(s32[3072]{0:T(1024)S(1)} %bitcast.354, s32[3072]{0:T(1024)} %add_select_fusion, s32[]{:T(128)} %constant.86.clone.1), kind=kCustom, calls=%fused_computation.167 | custom fusion | bytes 4608 | tf_op jit(solution)/shard_map/scatter | solution.py:154
  213.4 0.8 copy-done.1
  214.3 2.1 fusion.8
  216.4 6.0 %gather_fusion = bf16[1024,2048]{1,0:T(8,128)(2,1)} fusion(bf16[512,2048]{1,0:T(8,128)(2,1)S(1)} %fusion.8, s32[1024]{0:T(1024)S(1)} %maximum_clamp_fusion), kind=kCustom, calls=%fused_computation | custom fusion | bytes 8392704 | tf_op jit(solution)/shard_map/gather | solution.py:156
  222.5 2.5 broadcast_select_fusion
  225.0 55.9 %all_to_all.30 = bf16[16,1,64,2048]{3,2,1,0:T(8,128)(2,1)S(1)} all-to-all(bf16[16,1,64,2048]{3,2,1,0:T(8,128)(2,1)S(1)} %broadcast_select_fusion), channel_id=1, replica_groups=mesh['seq'=16,'hid'=16] {'seq'}, dimensions={0} | all-to-all | bytes 8388608 | tf_op jit(solution)/shard_map/all_to_all | solution.py:159
  280.9 2.0 copy-done.3
  282.9 3.6 fusion.11
  286.4 8.4 %convert_bitcast_fusion.1 = bf16[16,1,16,64,128]{4,3,0,2,1:T(8,128)(2,1)} fusion(bf16[352,2048]{1,0:T(8,128)(2,1)S(1)} %copy-done, bf16[16,1,64,2048]{3,2,1,0:T(8,128)(2,1)} %copy-done.3, f32[16,64,352]{2,1,0:T(8,128)} %fusion.11, bf16[352,2048]{1,0:T(8,128)(2,1)} %param.26), kind=kOutput, calls=%fused_computation.22 | convolution fusion | flops 2957049856 | bytes 12713984 | tf_op jit(solution)/shard_map/sicf,ifnx->niscx/dot_general | solution.py:168
  294.8 5.5 %copy.169 = bf16[16,1,16,64,128]{4,3,2,0,1:T(8,128)(2,1)} copy(bf16[16,1,16,64,128]{4,3,0,2,1:T(8,128)(2,1)} %convert_bitcast_fusion.1) | data formatting | bytes 8388608 | tf_op jit(solution)/shard_map/convert_element_type | solution.py:170
  300.3 9.6 %all-to-all-start.4 = ((bf16[16,1,1024,128]{3,2,1,0:T(8,128)(2,1)}), bf16[16,1,1024,128]{3,2,1,0:T(8,128)(2,1)}, u32[]{:S(2)}, u32[]{:S(2)}) async-start(bf16[16,1,1024,128]{3,2,1,0:T(8,128)(2,1)} %bitcast.344), calls=%async_computation.4 | async-start | bytes 8388608 | tf_op jit(solution)/shard_map/all_to_all | solution.py:172
  310.0 2.7 fusion.110
  312.7 4.4 fusion.14
  317.1 2.2 copy.212
  319.3 4.6 fusion.108
  324.5 1.4 copy-done.4
  325.8 72.9 %all-to-all-done.4 = bf16[16,1,1024,128]{3,2,1,0:T(8,128)(2,1)} async-done(((bf16[16,1,1024,128]{3,2,1,0:T(8,128)(2,1)}), bf16[16,1,1024,128]{3,2,1,0:T(8,128)(2,1)}, u32[]{:S(2)}, u32[]{:S(2)}) %all-to-all-start.4) | async-done | bytes 4194336 | tf_op jit(solution)/shard_map/all_to_all | solution.py:172
  398.7 13.2 %all-to-all-start.2 = ((bf16[16,512,1,128]{3,1,2,0:T(8,128)(2,1)}), bf16[16,512,1,128]{3,1,2,0:T(8,128)(2,1)S(1)}, u32[]{:S(2)}, u32[]{:S(2)}) async-start(bf16[16,512,1,128]{3,1,2,0:T(8,128)(2,1)} %copy-done.4), calls=%async_computation.2 | async-start | bytes 4194304 | tf_op jit(solution)/shard_map/all_to_all | solution.py:22
  411.9 2.9 bitcast_reduce_fusion
  414.8 1.1 copy.171
  415.8 28.3 %all-to-all-done.2 = bf16[16,512,1,128]{3,1,2,0:T(8,128)(2,1)S(1)} async-done(((bf16[16,512,1,128]{3,1,2,0:T(8,128)(2,1)}), bf16[16,512,1,128]{3,1,2,0:T(8,128)(2,1)S(1)}, u32[]{:S(2)}, u32[]{:S(2)}) %all-to-all-start.2) | async-done | bytes 2097184 | tf_op jit(solution)/shard_map/all_to_all | solution.py:22
  444.1 46.1 %all-to-all-start.5 = ((bf16[4,16,64,128]{3,2,0,1:T(8,128)(2,1)}), bf16[4,16,64,128]{3,2,0,1:T(8,128)(2,1)}, u32[]{:S(2)}, u32[]{:S(2)}) async-start(bf16[4,16,64,128]{3,2,0,1:T(8,128)(2,1)} %copy.171), calls=%async_computation.5 | async-start | bytes 2097152 | tf_op jit(solution)/shard_map/all_to_all | solution.py:180
  490.2 1.7 copy.174
  492.5 1.0 convert_reduce_fusion
  493.5 13.3 %all-to-all-done.5 = bf16[4,16,64,128]{3,2,0,1:T(8,128)(2,1)} async-done(((bf16[4,16,64,128]{3,2,0,1:T(8,128)(2,1)}), bf16[4,16,64,128]{3,2,0,1:T(8,128)(2,1)}, u32[]{:S(2)}, u32[]{:S(2)}) %all-to-all-start.5) | async-done | bytes 1048608 | tf_op jit(solution)/shard_map/all_to_all | solution.py:180
  506.8 1.3 copy.172
  508.2 9.2 %gather_fusion.1 = bf16[3072,128]{1,0:T(8,128)(2,1)S(1)} fusion(bf16[4096,128]{1,0:T(8,128)(2,1)S(1)} %bitcast.340, s32[3072]{0:T(1024)S(1)} %copy-done.14), kind=kCustom, calls=%fused_computation.1 | custom fusion | bytes 1585152 | tf_op jit(solution)/shard_map/gather | solution.py:188
  517.3 1.2 reshape.418
  518.6 1.9 fusion.111
  520.5 1.6 add_convert_fusion
  (101 shorter events, 17.9 us)
Async XLA Ops:
  0.0 286.4 %copy-start = (bf16[352,2048]{1,0:T(8,128)(2,1)S(1)}, bf16[352,2048]{1,0:T(8,128)(2,1)}, u32[]{:S(2)}) copy-start(bf16[352,2048]{1,0:T(8,128)(2,1)} %param.25) | copy-start | bytes 4325380
  2.0 22.9 %collective-permute-start = (bf16[512,2,128]{2,0,1:T(8,128)(2,1)S(1)}, bf16[512,2,128]{2,0,1:T(8,128)(2,1)S(1)}, u32[]{:S(2)}, u32[]{:S(2)}) collective-permute-start(bf16[512,2,128]{2,0,1:T(8,128)(2,1)S(1)} %constant_dynamic-update-slice_fusion), channel_id=1, source_target_pairs={{0,128},{16,144},{32,160},{48,176},{64,192},{80,208},{96,224},{112... | collective-permute-start | bytes 786440 | tf_op jit(solution)/shard_map/ppermute | solution.py:82
  6.9 20.0 %collective-permute-start.1 = (bf16[512,2,128]{2,0,1:T(8,128)(2,1)S(1)}, bf16[512,2,128]{2,0,1:T(8,128)(2,1)S(1)}, u32[]{:S(2)}, u32[]{:S(2)}) collective-permute-start(bf16[512,2,128]{2,0,1:T(8,128)(2,1)S(1)} %constant_dynamic-update-slice_fusion), channel_id=1, source_target_pairs={{0,112},{16,128},{32,144},{48,160},{64,176},{80,192},{96,208},{112... | collective-permute-start | bytes 786440 | tf_op jit(solution)/shard_map/ppermute | solution.py:82
  9.9 21.0 %collective-permute-start.2 = (bf16[512,2,128]{2,0,1:T(8,128)(2,1)S(1)}, bf16[512,2,128]{2,0,1:T(8,128)(2,1)S(1)}, u32[]{:S(2)}, u32[]{:S(2)}) collective-permute-start(bf16[512,2,128]{2,0,1:T(8,128)(2,1)S(1)} %constant_dynamic-update-slice_fusion), channel_id=1, source_target_pairs={{0,96},{16,112},{32,128},{48,144},{64,160},{80,176},{96,192},{112,... | collective-permute-start | bytes 786440 | tf_op jit(solution)/shard_map/ppermute | solution.py:82
  12.1 29.6 %collective-permute-start.3 = (bf16[512,2,128]{2,0,1:T(8,128)(2,1)S(1)}, bf16[512,2,128]{2,0,1:T(8,128)(2,1)S(1)}, u32[]{:S(2)}, u32[]{:S(2)}) collective-permute-start(bf16[512,2,128]{2,0,1:T(8,128)(2,1)S(1)} %constant_dynamic-update-slice_fusion), channel_id=1, source_target_pairs={{0,80},{16,96},{32,112},{48,128},{64,144},{80,160},{96,176},{112,1... | collective-permute-start | bytes 786440 | tf_op jit(solution)/shard_map/ppermute | solution.py:82
  13.4 33.9 %collective-permute-start.4 = (bf16[512,2,128]{2,0,1:T(8,128)(2,1)S(1)}, bf16[512,2,128]{2,0,1:T(8,128)(2,1)S(1)}, u32[]{:S(2)}, u32[]{:S(2)}) collective-permute-start(bf16[512,2,128]{2,0,1:T(8,128)(2,1)S(1)} %constant_dynamic-update-slice_fusion), channel_id=1, source_target_pairs={{0,64},{16,80},{32,96},{48,112},{64,128},{80,144},{96,160},{112,17... | collective-permute-start | bytes 786440 | tf_op jit(solution)/shard_map/ppermute | solution.py:82
  15.8 34.0 %copy-start.11 = (s32[4608]{0:T(1024)}, s32[4608]{0:T(1024)S(1)}, u32[]{:S(2)}) copy-start(s32[4608]{0:T(1024)S(1)} %get-tuple-element.42) | copy-start | bytes 55300
  15.8 34.0 %copy-start.12 = (s32[4608]{0:T(1024)}, s32[4608]{0:T(1024)S(1)}, u32[]{:S(2)}) copy-start(s32[4608]{0:T(1024)S(1)} %get-tuple-element.43) | copy-start | bytes 55300
  16.6 30.9 %copy-start.8 = (bf16[512,1,128]{2,0,1:T(8,128)(2,1)S(1)}, bf16[512,1,128]{2,0,1:T(8,128)(2,1)}, u32[]{:S(2)}) copy-start(bf16[512,1,128]{2,0,1:T(8,128)(2,1)} %param.17) | copy-start | bytes 393220
  24.8 22.5 %collective-permute-start.5 = (bf16[512,2,128]{2,0,1:T(8,128)(2,1)S(1)}, bf16[512,2,128]{2,0,1:T(8,128)(2,1)S(1)}, u32[]{:S(2)}, u32[]{:S(2)}) collective-permute-start(bf16[512,2,128]{2,0,1:T(8,128)(2,1)S(1)} %constant_dynamic-update-slice_fusion), channel_id=1, source_target_pairs={{0,48},{16,64},{32,80},{48,96},{64,112},{80,128},{96,144},{112,160... | collective-permute-start | bytes 786440 | tf_op jit(solution)/shard_map/ppermute | solution.py:82
  26.9 20.7 %copy-start.9 = (bf16[512,1,128]{2,0,1:T(8,128)(2,1)S(1)}, bf16[512,1,128]{2,0,1:T(8,128)(2,1)}, u32[]{:S(2)}) copy-start(bf16[512,1,128]{2,0,1:T(8,128)(2,1)} %param.18) | copy-start | bytes 393220
  26.9 20.7 %copy-start.20 = (bf16[512,1,128]{2,0,1:T(8,128)(2,1)S(1)}, bf16[512,1,128]{2,0,1:T(8,128)(2,1)}, u32[]{:S(2)}) copy-start(bf16[512,1,128]{2,0,1:T(8,128)(2,1)} %param.16) | copy-start | bytes 393220
  26.9 20.5 %collective-permute-start.6 = (bf16[512,2,128]{2,0,1:T(8,128)(2,1)S(1)}, bf16[512,2,128]{2,0,1:T(8,128)(2,1)S(1)}, u32[]{:S(2)}, u32[]{:S(2)}) collective-permute-start(bf16[512,2,128]{2,0,1:T(8,128)(2,1)S(1)} %constant_dynamic-update-slice_fusion), channel_id=1, source_target_pairs={{0,32},{16,48},{32,64},{48,80},{64,96},{80,112},{96,128},{112,144}... | collective-permute-start | bytes 786440 | tf_op jit(solution)/shard_map/ppermute | solution.py:82
  31.0 16.5 %collective-permute-start.7 = (bf16[512,2,128]{2,0,1:T(8,128)(2,1)S(1)}, bf16[512,2,128]{2,0,1:T(8,128)(2,1)S(1)}, u32[]{:S(2)}, u32[]{:S(2)}) collective-permute-start(bf16[512,2,128]{2,0,1:T(8,128)(2,1)S(1)} %constant_dynamic-update-slice_fusion), channel_id=1, source_target_pairs={{0,16},{16,32},{32,48},{48,64},{64,80},{80,96},{96,112},{112,128},... | collective-permute-start | bytes 786440 | tf_op jit(solution)/shard_map/ppermute | solution.py:82
  47.6 2.2 copy-start.15
  49.8 3.7 copy-start.2
  81.5 56.1 %all-to-all-start = ((bf16[16,512,1,128]{3,1,2,0:T(8,128)(2,1)}), bf16[16,512,1,128]{3,1,2,0:T(8,128)(2,1)S(1)}, u32[]{:S(2)}, u32[]{:S(2)}) async-start(bf16[16,512,1,128]{3,1,2,0:T(8,128)(2,1)} %fusion.77), calls=%async_computation | async-start | bytes 4194304 | tf_op jit(solution)/shard_map/all_to_all | solution.py:22
  137.9 0.7 copy-start.5
  141.3 7.4 %copy-start.16 = (s32[512,6]{0,1:T(8,128)S(1)}, s32[512,6]{0,1:T(8,128)}, u32[]{:S(2)}) copy-start(s32[512,6]{0,1:T(8,128)} %param.22) | copy-start | bytes 36868
  141.3 71.6 %all-to-all-start.1 = ((bf16[512,16,128]{2,0,1:T(8,128)(2,1)}), bf16[512,16,128]{2,0,1:T(8,128)(2,1)S(1)}, u32[]{:S(2)}, u32[]{:S(2)}) async-start(bf16[512,16,128]{2,0,1:T(8,128)(2,1)} %broadcast_in_dim.58), calls=%async_computation.1 | async-start | bytes 4194304 | tf_op jit(solution)/shard_map/all_to_all | solution.py:116
  212.2 2.0 copy-start.17
  212.9 1.3 copy-start.1
  216.4 6.0 %copy-start.18 = (pred[16,64]{1,0:T(8,128)(4,1)S(1)}, pred[16,64]{1,0:T(8,128)(4,1)}, u32[]{:S(2)}) copy-start(pred[16,64]{1,0:T(8,128)(4,1)} %broadcast_in_dim.61) | copy-start | bytes 3076
  225.0 57.9 %copy-start.19 = (bf16[352,2048]{1,0:T(8,128)(2,1)S(1)}, bf16[352,2048]{1,0:T(8,128)(2,1)}, u32[]{:S(2)}) copy-start(bf16[352,2048]{1,0:T(8,128)(2,1)} %param.24) | copy-start | bytes 4325380
  280.9 2.0 copy-start.3
  300.3 98.4 %all-to-all-start.4 = ((bf16[16,1,1024,128]{3,2,1,0:T(8,128)(2,1)}), bf16[16,1,1024,128]{3,2,1,0:T(8,128)(2,1)}, u32[]{:S(2)}, u32[]{:S(2)}) async-start(bf16[16,1,1024,128]{3,2,1,0:T(8,128)(2,1)} %bitcast.344), calls=%async_computation.4 | async-start | bytes 8388608 | tf_op jit(solution)/shard_map/all_to_all | solution.py:172
  324.5 1.4 copy-start.4
  398.7 45.4 %all-to-all-start.2 = ((bf16[16,512,1,128]{3,1,2,0:T(8,128)(2,1)}), bf16[16,512,1,128]{3,1,2,0:T(8,128)(2,1)S(1)}, u32[]{:S(2)}, u32[]{:S(2)}) async-start(bf16[16,512,1,128]{3,1,2,0:T(8,128)(2,1)} %copy-done.4), calls=%async_computation.2 | async-start | bytes 4194304 | tf_op jit(solution)/shard_map/all_to_all | solution.py:22
  414.7 77.2 %copy-start.13 = (s32[3072,1]{0,1:T(1,128)S(1)}, s32[3072,1]{0,1:T(1,128)}, u32[]{:S(2)}) copy-start(s32[3072,1]{0,1:T(1,128)} %get-tuple-element.5) | copy-start | bytes 36868
  444.1 62.7 %all-to-all-start.5 = ((bf16[4,16,64,128]{3,2,0,1:T(8,128)(2,1)}), bf16[4,16,64,128]{3,2,0,1:T(8,128)(2,1)}, u32[]{:S(2)}, u32[]{:S(2)}) async-start(bf16[4,16,64,128]{3,2,0,1:T(8,128)(2,1)} %copy.171), calls=%async_computation.5 | async-start | bytes 2097152 | tf_op jit(solution)/shard_map/all_to_all | solution.py:180
  492.5 15.6 %copy-start.14 = (s32[3072]{0:T(1024)S(1)}, s32[3072]{0:T(1024)}, u32[]{:S(2)}) copy-start(s32[3072]{0:T(1024)} %broadcast_clamp_fusion) | copy-start | bytes 36868
  508.2 10.4 %copy-start.10 = (bf16[512,6,1]{1,2,0:T(2,128)(2,1)S(1)}, bf16[512,6,1]{1,2,0:T(2,128)(2,1)}, u32[]{:S(2)}) copy-start(bf16[512,6,1]{1,2,0:T(2,128)(2,1)} %copy.174) | copy-start | bytes 18436
  517.3 3.2 copy-start.6
  517.3 3.2 copy-start.7
